TPU v7x, 32 devices: a whole 2x2x4 slice. The times are simulated.
32 devices in a mesh: groups: 2 (over y), expert: 4 (over z), dp: 4 (over x, core).
Axes of the slice: x: 2, y: 2, z: 4, core: 2. Of those that a mesh axis runs over, the one named last changes fastest.
Arguments:
- out_grad: bfloat16 [4096, 2048], P(('groups', 'expert', 'dp')), parts along dimension 0, may hold values from -0.5 to 0.5
- gate_weights: bfloat16 [4096, 8], P(('groups', 'expert', 'dp')), parts along dimension 0, may hold values from 0.049804688 to 0.5
- expert_ids: int32 [4096, 8], P(('groups', 'expert', 'dp')), parts along dimension 0, may hold values from 0 to 31, all different within a row; in each aligned block of 128 rows (0 to 127, 128 to 255, ...) at most 36 rows name the same one
- hidden: bfloat16 [32, 8, 4, 36, 768], P('expert', ('groups', 'dp')), parts along dimension 1, may hold values from -6 to 6
- down_weight: bfloat16 [32, 768, 2048], P('expert', None, 'dp'), may hold values from -0.21875 to 0.21875
Outputs:
- weight_grad: float32 [64, 768, 2048], P(('groups', 'expert'), None, 'dp'), parts along dimension 0
- gate_grad: float32 [4096, 8], P(('groups', 'expert', 'dp')), parts along dimension 0
There are 2 independent parts, one for each index of `groups`. A program takes and returns all parts, laid end to end along the dimension named above; an argument that names none is the same for every part. Nothing has to cross between parts.
Inputs may be any that keep to these rules, and one draw needn't show every extreme that they name: `expert_ids`: each token names 8 different experts; within each block of 128 tokens (one device's tokens) no expert is named by more than 36 tokens, a bound that some block reaches.
All inputs are finite; a program needn't handle non-finite values.
Results may differ from a plain program's by a relative error of at most 0.0095.
Values may be sent and summed in bfloat16 or wider, within the bound.
No kernel may reach another device: no remote copies, remote signals or barrier semaphores. Data moves between devices by JAX's collectives and lax.ppermute only.
A program may use at most 128 MiB of HBM per device.

v0:
```python
import jax
import jax.numpy as jnp
from jax import lax
from jax.sharding import PartitionSpec as P


def per_device(out_grad, gate_weights, expert_ids, hidden, down_weight):
    tok_rows, top_count = expert_ids.shape
    row_width = out_grad.shape[1]
    local_count = hidden.shape[0]
    capacity = hidden.shape[3]
    peer_count = lax.axis_size("expert")
    shards = lax.axis_size("dp")
    expert_count = local_count * peer_count
    col_width = row_width // shards
    block_count = peer_count * shards
    f32 = jnp.float32
    bf16 = jnp.bfloat16
    my_dp = lax.axis_index("dp")
    fetched = lax.ppermute(hidden, "dp", [(j, j ^ 2) for j in range(shards)])
    paired = lax.ppermute(
        jnp.concatenate([hidden, fetched], axis=1), "dp", [(j, j ^ 1) for j in range(shards)]
    )
    pieces = [hidden, fetched, paired[:, 0:1], paired[:, 1:2]]
    piece_replica = [my_dp, my_dp ^ 2, my_dp ^ 1, my_dp ^ 3]
    meta = jnp.concatenate([expert_ids.astype(bf16), gate_weights], axis=1).reshape(-1)
    meta_len = meta.shape[0]
    meta_rows = -(-meta_len // col_width)
    meta = jnp.pad(meta, (0, meta_rows * col_width - meta_len)).reshape(meta_rows, 1, col_width)
    cols = out_grad.reshape(tok_rows, shards, col_width)
    cols = jnp.concatenate([cols, jnp.broadcast_to(meta, (meta_rows, shards, col_width))], axis=0)
    cols = lax.all_to_all(cols, "dp", split_axis=1, concat_axis=0, tiled=True)
    cols = cols.reshape(shards, tok_rows + meta_rows, col_width)
    got = lax.all_gather(cols, "expert", axis=0, tiled=False)
    got = got.reshape(block_count, tok_rows + meta_rows, col_width)
    grad_all = got[:, :tok_rows]
    meta_all = got[:, tok_rows:].reshape(block_count, meta_rows * col_width)[:, :meta_len]
    meta_all = meta_all.reshape(block_count, tok_rows, 2 * top_count)
    ids_all = meta_all[:, :, :top_count].astype(jnp.int32)
    gate_all = meta_all[:, :, top_count:]
    my_experts = lax.axis_index("expert") * local_count + jnp.arange(local_count, dtype=jnp.int32)
    hit = ids_all[:, :, :, None] == my_experts[None, None, None, :]
    chose = jnp.any(hit, axis=2)
    gate_hit = jnp.sum(jnp.where(hit, gate_all.astype(f32)[:, :, :, None], 0.0), axis=2)
    before = (jnp.arange(tok_rows)[:, None] < jnp.arange(tok_rows)[None, :]).astype(bf16)
    rank = jnp.einsum("bul,ut->btl", chose.astype(bf16), before, preferred_element_type=f32).astype(
        jnp.int32
    )
    slot_ids = jnp.arange(capacity, dtype=jnp.int32)
    chose_t = chose.transpose(0, 2, 1)
    rank_t = rank.transpose(0, 2, 1)
    gate_t = gate_hit.transpose(0, 2, 1)
    select = chose_t[:, :, None, :] & (rank_t[:, :, None, :] == slot_ids[None, None, :, None])
    select_gate = jnp.where(select, gate_t[:, :, None, :], 0.0).astype(bf16)
    grad_rows = jnp.einsum(
        "blct,btd->blcd", select.astype(bf16), grad_all, preferred_element_type=f32
    ).astype(bf16)
    scaled = jnp.einsum("blct,btd->blcd", select_gate, grad_all, preferred_element_type=f32).astype(
        bf16
    )
    grad_rows = grad_rows.reshape(peer_count, shards, local_count, capacity, col_width)
    scaled = scaled.reshape(peer_count, shards, local_count, capacity, col_width)
    weight_grad = None
    slot_part = jnp.zeros((peer_count, shards, local_count, capacity), f32)
    for piece, replica in zip(pieces, piece_replica):
        piece = piece[:, 0]
        scaled_r = lax.dynamic_index_in_dim(scaled, replica, axis=1, keepdims=False)
        rows_r = lax.dynamic_index_in_dim(grad_rows, replica, axis=1, keepdims=False)
        part = (
            jnp.einsum("lscf,slcd->lfd", piece, scaled_r, preferred_element_type=f32)
            .astype(bf16)
            .astype(f32)
        )
        weight_grad = part if weight_grad is None else weight_grad + part
        expert_out = jnp.einsum("lscf,lfd->slcd", piece, down_weight, preferred_element_type=f32)
        slot_r = jnp.sum(rows_r.astype(f32) * expert_out, axis=3)
        slot_part = lax.dynamic_update_index_in_dim(slot_part, slot_r, replica, axis=1)
    send_back = slot_part.reshape(block_count, local_count, capacity)
    returned = lax.all_to_all(send_back, ("expert", "dp"), split_axis=0, concat_axis=0, tiled=True)
    returned = returned.reshape(peer_count, shards, local_count, capacity)
    slot_grad = jnp.sum(returned, axis=1).reshape(expert_count, capacity)
    own_hit = expert_ids[:, :, None] == jnp.arange(expert_count, dtype=jnp.int32)[None, None, :]
    own_chose = jnp.any(own_hit, axis=1)
    own_rank = jnp.einsum(
        "ue,ut->te", own_chose.astype(bf16), before, preferred_element_type=f32
    ).astype(jnp.int32)
    own_slot = jnp.sum(jnp.where(own_hit, own_rank[:, None, :], 0), axis=2)
    by_slot = jnp.sum(jnp.where(own_hit[:, :, :, None], slot_grad[None, None], 0.0), axis=2)
    gate_grad = jnp.sum(
        jnp.where(own_slot[:, :, None] == slot_ids[None, None, :], by_slot, 0.0), axis=2
    )
    return (weight_grad, gate_grad)


def solution(mesh):
    return jax.shard_map(
        per_device,
        mesh=mesh,
        in_specs=(
            P(("groups", "expert", "dp"), None),
            P(("groups", "expert", "dp"), None),
            P(("groups", "expert", "dp"), None),
            P("expert", ("groups", "dp"), None, None, None),
            P("expert", None, "dp"),
        ),
        out_specs=(P(("groups", "expert"), None, "dp"), P(("groups", "expert", "dp"), None)),
        check_vma=False,
    )
```

profile of v0, /device:TPU:0, one launch (start us, length us, event | category | flops | bytes accessed | tf_op | source)
XLA Modules:
  0.0 151.6 jit_solution(17778870522974405558)
XLA Ops:
  9.0 1.3 copy.186
  11.1 13.3 %all_to_all.20 = bf16[132,4,512]{2,0,1:T(8,128)(2,1)} all-to-all(bf16[132,4,512]{2,0,1:T(8,128)(2,1)S(1)} %copy.189), channel_id=1, replica_groups=mesh['groups'=2,'expert'=4,'dp'=4] {'dp'}, dimensions={1} | all-to-all | bytes 1081344 | tf_op jit(solution)/shard_map/all_to_all | solution.py:32
  24.4 2.0 %copy.196 = bf16[8,1,4,36,768]{4,0,3,2,1:T(8,128)(2,1)S(1)} copy(bf16[8,1,4,36,768]{4,2,3,1,0:T(4,128)(2,1)} %param.8) | data formatting | bytes 3538944 | tf_op args[3]
  27.7 39.3 %collective-permute-done = bf16[8,1,4,36,768]{4,0,3,2,1:T(8,128)(2,1)S(1)} collective-permute-done((bf16[8,1,4,36,768]{4,0,3,2,1:T(8,128)(2,1)S(1)}, bf16[8,1,4,36,768]{4,0,3,2,1:T(8,128)(2,1)S(1)}, u32[]{:S(2)}, u32[]{:S(2)}) %collective-permute-start) | collective-permute-done | bytes 1769504 | tf_op jit(solution)/shard_map/ppermute | solution.py:20
  67.0 2.3 %pad_maximum_fusion = bf16[8,2,4,36,768]{4,0,3,2,1:T(8,128)(2,1)} fusion(bf16[8,1,4,36,768]{4,0,3,2,1:T(8,128)(2,1)S(1)} %collective-permute-done, bf16[8,1,4,36,768]{4,0,3,2,1:T(8,128)(2,1)S(1)} %copy.196), kind=kLoop, calls=%fused_computation.15 | loop fusion | flops 1769472 | bytes 7077888 | tf_op jit(solution)/shard_map/concatenate | solution.py:22
  69.3 4.3 %all-gather.3.cloned.1.call-done = bf16[16,132,1,512]{3,1,2,0:T(8,128)(2,1)} async-done(((bf16[4,132,1,512]{3,1,2,0:T(8,128)(2,1)}), bf16[16,132,1,512]{3,1,2,0:T(8,128)(2,1)}) %all-gather.3.cloned.1.call-update) | async-done | bytes 2162704 | tf_op jit(solution)/shard_map/all_gather | solution.py:34
  75.0 1.0 fusion.56
  76.0 1.2 copy.226
  77.9 1.5 convolution_convert_fusion.1
  79.5 1.5 %convolution_convert_fusion = bf16[16,8,36,512]{3,2,1,0:T(8,128)(2,1)S(1)} fusion(bf16[16,132,512]{2,1,0:T(8,128)(2,1)S(1)} %bitcast.135, bf16[16,8,128]{2,1,0:T(8,128)(2,1)S(1)} %bitcast.142, s32[16,8,128]{2,1,0:T(8,128)S(1)} %convolution_convert_fusion.2, pred[16,8,128]{2,1,0:T(8,128)(4,1)S(1)} %bitcast.141), kind=kOutput, calls=%fused_computation.16 | convolution fusion | flops 608108544 | bytes 6930432 | tf_op jit(solution)/shard_map/blct,btd->blcd/dot_general | solution.py:58
  81.0 4.1 %constant_dynamic-slice_fusion = (bf16[4,1,8,36,512]{4,3,2,1,0:T(8,128)(2,1)}, bf16[4,1,8,36,512]{4,3,2,1,0:T(8,128)(2,1)}, bf16[4,1,8,36,512]{4,3,2,1,0:T(8,128...) fusion(bf16[4,4,8,36,512]{4,3,2,1,0:T(8,128)(2,1)S(1)} %bitcast, ...), kind=kLoop, calls=%fused_computation.78 | loop fusion | bytes 18874384 | tf_op jit(solution)/shard_map/jit(dynamic_index_in_dim)/dynamic_slice | solution.py:68
  85.1 5.0 %fusion.12 = f32[4,8,36]{2,0,1:T(4,128)S(1)} fusion(bf16[4,1,8,36,512]{4,3,2,1,0:T(8,128)(2,1)} %get-tuple-element.21, bf16[8,4,36,768]{3,1,2,0:T(4,128)(2,1)} %bitcast.138, bf16[8,768,512]{2,1,0:T(8,128)(2,1)} %param.9), kind=kOutput, calls=%fused_computation.25 | convolution fusion | flops 907737984 | bytes 9245184 | tf_op jit(solution)/shard_map/lscf,lfd->slcd/dot_general | solution.py:75
  91.4 4.3 %fusion.11 = f32[4,8,36]{2,0,1:T(4,128)S(1)} fusion(bf16[4,1,8,36,512]{4,3,2,1,0:T(8,128)(2,1)S(1)} %copy-done.10, bf16[8,1,4,36,768]{4,0,3,2,1:T(8,128)(2,1)S(1)} %copy-done.4, bf16[8,768,512]{2,1,0:T(8,128)(2,1)} %param.9), kind=kOutput, calls=%fused_computation.23 | convolution fusion | flops 907737984 | bytes 9245184 | tf_op jit(solution)/shard_map/lscf,lfd->slcd/dot_general | solution.py:75
  96.4 4.6 %fusion.22 = bf16[8,512,768,1]{2,1,3,0:T(8,128)(2,1)} fusion(bf16[8,4,36,768]{3,1,2,0:T(4,128)(2,1)S(1)} %bitcast.139, bf16[4,1,8,36,512]{4,3,2,1,0:T(8,128)(2,1)S(1)} %copy-done.9), kind=kOutput, calls=%fused_computation.39 | convolution fusion | flops 905969664 | bytes 9240576 | tf_op jit(solution)/shard_map/lscf,slcd->lfd/dot_general | solution.py:70
  101.0 2.3 %fusion.55 = (bf16[8,1,4,36,768]{4,0,3,2,1:T(8,128)(2,1)S(1)}, bf16[8,1,4,36,768]{4,0,3,2,1:T(8,128)(2,1)S(1)}) fusion(bf16[8,2,4,36,768]{4,0,3,2,1:T(8,128)(2,1)} %collective-permute-done.1), kind=kLoop, calls=%fused_computation.88 | loop fusion | bytes 7077888 | tf_op jit(solution)/shard_map/slice | solution.py:24
  103.4 1.6 %fusion.9 = f32[4,8,36]{2,0,1:T(4,128)S(1)} fusion(bf16[4,1,8,36,512]{4,3,2,1,0:T(8,128)(2,1)S(1)} %copy-done.8, bf16[8,768,512]{2,1,0:T(8,128)(2,1)S(1)} %bitcast.149, bf16[8,1,4,36,768]{4,0,3,2,1:T(8,128)(2,1)S(1)} %get-tuple-element.26), kind=kOutput, calls=%fused_computation.19 | convolution fusion | flops 907737984 | bytes 9245184 | tf_op jit(solution)/shard_map/lscf,lfd->slcd/dot_general | solution.py:75
  105.0 1.8 %fusion.10 = f32[4,8,36]{2,0,1:T(4,128)S(1)} fusion(bf16[4,1,8,36,512]{4,3,2,1,0:T(8,128)(2,1)S(1)} %copy-done.7, bf16[8,768,512]{2,1,0:T(8,128)(2,1)S(1)} %bitcast.149, bf16[8,1,4,36,768]{4,0,3,2,1:T(8,128)(2,1)S(1)} %get-tuple-element.27), kind=kOutput, calls=%fused_computation.21 | convolution fusion | flops 907737984 | bytes 9245184 | tf_op jit(solution)/shard_map/lscf,lfd->slcd/dot_general | solution.py:75
  108.0 1.6 %reshape.70 = f32[16,1,288]{2,1,0:T(1,128)} reshape(f32[16,8,36]{2,1,0:T(8,128)} %bitcast.43) | data formatting | bytes 36864
  109.5 4.1 %all-to-all-start.1 = ((f32[16,1,288]{2,1,0:T(1,128)}), f32[16,1,288]{2,1,0:T(1,128)}, u32[]{:S(2)}, u32[]{:S(2)}) async-start(f32[16,1,288]{2,1,0:T(1,128)} %reshape.70), calls=%async_computation.1 | async-start | bytes 49152 | tf_op jit(solution)/shard_map/all_to_all | solution.py:79
  113.7 3.4 %fusion.17 = bf16[8,768,512,1]{1,2,3,0:T(8,128)(2,1)S(1)} fusion(bf16[8,1,4,36,768]{4,0,3,2,1:T(8,128)(2,1)S(1)} %get-tuple-element.27, bf16[4,1,8,36,512]{4,3,2,1,0:T(8,128)(2,1)} %get-tuple-element.33), kind=kOutput, calls=%fused_computation.34 | convolution fusion | flops 905969664 | bytes 9240576 | tf_op jit(solution)/shard_map/lscf,slcd->lfd/dot_general | solution.py:70
  117.1 1.9 %fusion.18 = bf16[8,768,512,1]{1,2,3,0:T(8,128)(2,1)S(1)} fusion(bf16[8,1,4,36,768]{4,0,3,2,1:T(8,128)(2,1)S(1)} %get-tuple-element.26, bf16[4,1,8,36,512]{4,3,2,1,0:T(8,128)(2,1)S(1)} %copy-done), kind=kOutput, calls=%fused_computation.35 | convolution fusion | flops 905969664 | bytes 9240576 | tf_op jit(solution)/shard_map/lscf,slcd->lfd/dot_general | solution.py:70
  119.0 9.5 %fusion = f32[8,768,512]{1,2,0:T(8,128)} fusion(bf16[8,512,768,1]{2,1,3,0:T(8,128)(2,1)} %fusion.22, bf16[8,768,512,1]{1,2,3,0:T(8,128)(2,1)S(1)} %fusion.17, bf16[8,768,512,1]{1,2,3,0:T(8,128)(2,1)S(1)} %fusion.18, bf16[8,1,4,36,768]{4,0,3,2,1:T(8,128)(2,1)S(1)} %copy-done.5, bf16[4,1,8,36,512]{4,3,2,1,0:T(8,128)(2,1)} %get-tuple-element.35), kind=kOutput, calls=%fused_computation.3 | convolution fusion | flops 931135488 | bytes 34406400 | tf_op jit(solution)/shard_map/lscf,slcd->lfd/dot_general | solution.py:70
  128.5 12.6 %copy.216 = f32[8,768,512]{2,1,0:T(8,128)} copy(f32[8,768,512]{1,2,0:T(8,128)} %fusion) | data formatting | bytes 25165824
  141.6 1.4 reduce
  (68 shorter events, 11.2 us)
Async XLA Ops:
  7.2 66.5 %all-gather.3.cloned.1.call-start = ((), (), s32[]{:S(2)}) async-start(), calls=%async_computation.2 | async-start | bytes 2785280 | tf_op jit(solution)/shard_map/all_gather | solution.py:34
  24.4 2.5 %copy-start.12 = (s32[128,8]{0,1:T(8,128)S(1)}, s32[128,8]{0,1:T(8,128)}, u32[]{:S(2)}) copy-start(s32[128,8]{0,1:T(8,128)} %param.7) | copy-start | bytes 12292
  26.4 40.5 %collective-permute-start = (bf16[8,1,4,36,768]{4,0,3,2,1:T(8,128)(2,1)S(1)}, bf16[8,1,4,36,768]{4,0,3,2,1:T(8,128)(2,1)S(1)}, u32[]{:S(2)}, u32[]{:S(2)}) collective-permute-start(bf16[8,1,4,36,768]{4,0,3,2,1:T(8,128)(2,1)S(1)} %copy.196), channel_id=1, source_target_pairs={{0,2},{1,3},{2,0},{3,1},{4,6},{5,7},{6,4},{7,5},{8,10},{9,11},{10,... | collective-permute-start | bytes 5308424 | tf_op jit(solution)/shard_map/ppermute | solution.py:20
  67.0 2.4 %copy-start.3 = (bf16[8,1,4,36,768]{4,0,3,2,1:T(8,128)(2,1)}, bf16[8,1,4,36,768]{4,0,3,2,1:T(8,128)(2,1)S(1)}, u32[]{:S(2)}) copy-start(bf16[8,1,4,36,768]{4,0,3,2,1:T(8,128)(2,1)S(1)} %collective-permute-done) | copy-start | bytes 5308420
  69.3 31.7 %collective-permute-start.1 = (bf16[8,2,4,36,768]{4,0,3,2,1:T(8,128)(2,1)}, bf16[8,2,4,36,768]{4,0,3,2,1:T(8,128)(2,1)}, u32[]{:S(2)}, u32[]{:S(2)}) collective-permute-start(bf16[8,2,4,36,768]{4,0,3,2,1:T(8,128)(2,1)} %pad_maximum_fusion), channel_id=1, source_target_pairs={{0,1},{1,0},{2,3},{3,2},{4,5},{5,4},{6,7},{7,6},{8,9},{9,8},{10,11... | collective-permute-start | bytes 10616840 | tf_op jit(solution)/shard_map/ppermute | solution.py:21
  75.0 2.9 %copy-start.1 = (bf16[16,132,1,512]{3,1,2,0:T(8,128)(2,1)S(1)}, bf16[16,132,1,512]{3,1,2,0:T(8,128)(2,1)}, u32[]{:S(2)}) copy-start(bf16[16,132,1,512]{3,1,2,0:T(8,128)(2,1)} %all-gather.3.cloned.1.call-done) | copy-start | bytes 6488068
  77.9 1.6 %copy-start.2 = (bf16[16,132,1,512]{3,1,2,0:T(8,128)(2,1)S(1)}, bf16[16,132,1,512]{3,1,2,0:T(8,128)(2,1)}, u32[]{:S(2)}) copy-start(bf16[16,132,1,512]{3,1,2,0:T(8,128)(2,1)} %all-gather.3.cloned.1.call-done) | copy-start | bytes 6488068
  85.1 6.3 %copy-start.4 = (bf16[8,1,4,36,768]{4,0,3,2,1:T(8,128)(2,1)S(1)}, bf16[8,1,4,36,768]{4,0,3,2,1:T(8,128)(2,1)}, u32[]{:S(2)}) copy-start(bf16[8,1,4,36,768]{4,0,3,2,1:T(8,128)(2,1)} %copy-done.3) | copy-start | bytes 5308420
  85.1 6.3 %copy-start.10 = (bf16[4,1,8,36,512]{4,3,2,1,0:T(8,128)(2,1)S(1)}, bf16[4,1,8,36,512]{4,3,2,1,0:T(8,128)(2,1)}, u32[]{:S(2)}) copy-start(bf16[4,1,8,36,512]{4,3,2,1,0:T(8,128)(2,1)} %get-tuple-element.20) | copy-start | bytes 3538948
  91.4 5.0 %copy-start.6 = (bf16[8,1,4,36,768]{4,2,3,1,0:T(4,128)(2,1)S(1)}, bf16[8,1,4,36,768]{4,2,3,1,0:T(4,128)(2,1)}, u32[]{:S(2)}) copy-start(bf16[8,1,4,36,768]{4,2,3,1,0:T(4,128)(2,1)} %param.8) | copy-start | bytes 5308420
  91.4 5.0 %copy-start.9 = (bf16[4,1,8,36,512]{4,3,2,1,0:T(8,128)(2,1)S(1)}, bf16[4,1,8,36,512]{4,3,2,1,0:T(8,128)(2,1)}, u32[]{:S(2)}) copy-start(bf16[4,1,8,36,512]{4,3,2,1,0:T(8,128)(2,1)} %get-tuple-element.32) | copy-start | bytes 3538948
  91.4 12.0 %slice-start = ((s8[6291456]{0:T(1024)(128)(4,1)}), s8[2097152]{0:T(1024)(128)(4,1)S(1)}, s32[]{:S(2)}) async-start(s8[6291456]{0:T(1024)(128)(4,1)} %bitcast.148), calls=%async_computation.3 | async-start | bytes 4194304
  96.4 7.0 %slice-start.1 = ((s8[6291456]{0:T(1024)(128)(4,1)}), s8[4194304]{0:T(1024)(128)(4,1)S(1)}, s32[]{:S(2)}) async-start(s8[6291456]{0:T(1024)(128)(4,1)} %bitcast.148), calls=%async_computation.4 | async-start | bytes 8388608
  101.0 2.4 %copy-start.8 = (bf16[4,1,8,36,512]{4,3,2,1,0:T(8,128)(2,1)S(1)}, bf16[4,1,8,36,512]{4,3,2,1,0:T(8,128)(2,1)}, u32[]{:S(2)}) copy-start(bf16[4,1,8,36,512]{4,3,2,1,0:T(8,128)(2,1)} %get-tuple-element.18) | copy-start | bytes 3538948
  103.4 1.6 %copy-start.7 = (bf16[4,1,8,36,512]{4,3,2,1,0:T(8,128)(2,1)S(1)}, bf16[4,1,8,36,512]{4,3,2,1,0:T(8,128)(2,1)}, u32[]{:S(2)}) copy-start(bf16[4,1,8,36,512]{4,3,2,1,0:T(8,128)(2,1)} %get-tuple-element.19) | copy-start | bytes 3538948
  109.5 31.6 %all-to-all-start.1 = ((f32[16,1,288]{2,1,0:T(1,128)}), f32[16,1,288]{2,1,0:T(1,128)}, u32[]{:S(2)}, u32[]{:S(2)}) async-start(f32[16,1,288]{2,1,0:T(1,128)} %reshape.70), calls=%async_computation.1 | async-start | bytes 49152 | tf_op jit(solution)/shard_map/all_to_all | solution.py:79
  113.7 3.4 %copy-start = (bf16[4,1,8,36,512]{4,3,2,1,0:T(8,128)(2,1)S(1)}, bf16[4,1,8,36,512]{4,3,2,1,0:T(8,128)(2,1)}, u32[]{:S(2)}) copy-start(bf16[4,1,8,36,512]{4,3,2,1,0:T(8,128)(2,1)} %get-tuple-element.34) | copy-start | bytes 3538948
  117.1 2.0 %copy-start.5 = (bf16[8,1,4,36,768]{4,0,3,2,1:T(8,128)(2,1)S(1)}, bf16[8,1,4,36,768]{4,0,3,2,1:T(8,128)(2,1)}, u32[]{:S(2)}) copy-start(bf16[8,1,4,36,768]{4,0,3,2,1:T(8,128)(2,1)} %copy-done.3) | copy-start | bytes 5308420
  128.5 14.8 %copy-start.11 = (pred[128,8,32]{0,2,1:T(8,128)(4,1)S(1)}, pred[128,8,32]{0,2,1:T(8,128)(4,1)}, u32[]{:S(2)}) copy-start(pred[128,8,32]{0,2,1:T(8,128)(4,1)} %get-tuple-element.31) | copy-start | bytes 98308
Sparse Core Ops, SparseCore 0:
  24.6 49.0 all-gather.2
where the time goes:
time: 152 us
  waiting for transfers between devices  43.6 us (29%)
  matrix products  35.5 us (23%)
  local copies, waits for them, and re-layouts  32.5 us (21%)
  between operations  14.3 us (9%)
  blocking collectives  13.3 us (9%)
  other arithmetic  7.75 us (5%)
  starting transfers between devices  4.59 us (3%)
    ppermute x1, waiting for transfers between devices, per_device(): fetched = lax.ppermute(hidden, 'dp', [(j, j ^ 2) for j in range(shards)])  39.3 us
    dot_general x4, matrix products, per_device(): jnp.einsum('lscf,slcd->lfd', piece, scaled_r, preferred_element_type=f32)  19.4 us
    unnamed x37, local copies, waits for them, and re-layouts  19.2 us
    all_to_all x1, blocking collectives, per_device(): cols = lax.all_to_all(cols, 'dp', split_axis=1, concat_axis=0, tiled=True)  13.3 us
    dot_general x4, matrix products, per_device(): jnp.einsum('lscf,lfd->slcd', piece, down_weight, preferred_element_type=f32)  12.7 us
    all_gather x1, waiting for transfers between devices, per_device(): got = lax.all_gather(cols, 'expert', axis=0, tiled=False)  4.34 us
    all_to_all x1, starting transfers between devices, per_device(): lax.all_to_all(send_back, ('expert', 'dp'), split_axis=0, concat_axis=0,...  4.13 us
    dynamic_slice x1, local copies, waits for them, and re-layouts, per_device(): lax.dynamic_index_in_dim(grad_rows, replica, axis=1, keepdims=False)  4.08 us
  transfers between devices with their start and end apart: 4, of which 2 were waited for; matrix products, arithmetic and copies ran while one was open for 39% of the time, Pallas kernels for 0%

commit v1 on v0

--- a/solution.py
+++ b/solution.py
@@ -2,6 +2,18 @@
 import jax.numpy as jnp
 from jax import lax
 from jax.sharding import PartitionSpec as P
+
+
+def cut_along(array, dim, length):
+    lengths = array.shape
+    blocks = array.reshape(*lengths[:dim], length, lengths[dim] // length, *lengths[dim + 1 :])
+    return jnp.moveaxis(blocks, dim, 0)
+
+
+def in_order(blocks, dim):
+    lengths = list(blocks.shape[1:])
+    lengths[dim] *= blocks.shape[0]
+    return jnp.moveaxis(blocks, 0, dim).reshape(lengths)
 
 
 def per_device(out_grad, gate_weights, expert_ids, hidden, down_weight):
@@ -29,7 +41,15 @@
     meta = jnp.pad(meta, (0, meta_rows * col_width - meta_len)).reshape(meta_rows, 1, col_width)
     cols = out_grad.reshape(tok_rows, shards, col_width)
     cols = jnp.concatenate([cols, jnp.broadcast_to(meta, (meta_rows, shards, col_width))], axis=0)
-    cols = lax.all_to_all(cols, "dp", split_axis=1, concat_axis=0, tiled=True)
+    peers, position = (lax.axis_size("dp"), lax.axis_index("dp"))
+    blocks = cut_along(cols, 1, peers)
+    out = blocks
+    for step in range(1, peers):
+        target, source = ((position + step) % peers, (position - step) % peers)
+        sent = lax.dynamic_index_in_dim(blocks, target, 0)
+        other = lax.ppermute(sent, "dp", [(i, (i + step) % peers) for i in range(peers)])
+        out = lax.dynamic_update_slice_in_dim(out, other, source, axis=0)
+    cols = in_order(out, 0)
     cols = cols.reshape(shards, tok_rows + meta_rows, col_width)
     got = lax.all_gather(cols, "expert", axis=0, tiled=False)
     got = got.reshape(block_count, tok_rows + meta_rows, col_width)

time: 152 us -> 152 us (level)
  blocking collectives: 13.3 us -> 0 us
  starting transfers between devices: 4.59 us -> 10.1 us
  local copies, waits for them, and re-layouts: 32.5 us -> 35.3 us
  waiting for transfers between devices: 43.6 us -> 46.2 us
  matrix products: 35.5 us -> 37.1 us
    all_to_all x1 -> x0, blocking collectives: 13.3 us -> none  [per_device(): cols = lax.all_to_all(cols, 'dp', split_axis=1, concat_axis=0, tiled=True)]
    ppermute x0 -> x3, starting transfers between devices: none -> 4.84 us  [per_device(): lax.ppermute(sent, 'dp', [(i, (i + step) % peers) for i in range(peers)])]
    ppermute x0 -> x3, waiting for transfers between devices: none -> 3.78 us  [per_device(): lax.ppermute(sent, 'dp', [(i, (i + step) % peers) for i in range(peers)])]
    all_gather x0 -> x1, local copies, waits for them, and re-layouts: none -> 2.03 us  [per_device(): got = lax.all_gather(cols, 'expert', axis=0, tiled=False)]
    dot_general x1, matrix products: 1.52 us -> 3.13 us  [per_device(): jnp.einsum('blct,btd->blcd', select_gate, grad_all, preferred_element_typ...]
    unnamed x37 -> x35, local copies, waits for them, and re-layouts: 19.2 us -> 19.1 us
  transfers between devices with their start and end apart: 4 -> 7, of which waited for: 2 -> 4; matrix products, arithmetic and copies ran while one was open for 39% -> 42% of each run, Pallas kernels for 0% -> 0%
where the time goes in v1:
time: 152 us; the launch traced here: 151 us
  waiting for transfers between devices  46.2 us (30%)
  matrix products  37.1 us (24%)
  local copies, waits for them, and re-layouts  35.3 us (23%)
  between operations  14.4 us (9%)
  starting transfers between devices  10.1 us (7%)
  other arithmetic  7.92 us (5%)
    ppermute x1, waiting for transfers between devices, per_device(): fetched = lax.ppermute(hidden, 'dp', [(j, j ^ 2) for j in range(shards)])  38.8 us
    dot_general x4, matrix products, per_device(): jnp.einsum('lscf,slcd->lfd', piece, scaled_r, preferred_element_type=f32)  19.4 us
    unnamed x35, local copies, waits for them, and re-layouts  19.1 us
    dot_general x4, matrix products, per_device(): jnp.einsum('lscf,lfd->slcd', piece, down_weight, preferred_element_type=f32)  12.7 us
    ppermute x3, starting transfers between devices, per_device(): lax.ppermute(sent, 'dp', [(i, (i + step) % peers) for i in range(peers)])  4.84 us
    all_to_all x1, starting transfers between devices, per_device(): lax.all_to_all(send_back, ('expert', 'dp'), split_axis=0, concat_axis=0,...  4.13 us
    dynamic_slice x1, local copies, waits for them, and re-layouts, per_device(): lax.dynamic_index_in_dim(grad_rows, replica, axis=1, keepdims=False)  4.08 us
    ppermute x3, waiting for transfers between devices, per_device(): lax.ppermute(sent, 'dp', [(i, (i + step) % peers) for i in range(peers)])  3.78 us
  transfers between devices with their start and end apart: 7, of which 4 were waited for; matrix products, arithmetic and copies ran while one was open for 42% of the time, Pallas kernels for 0%

profile of v1, /device:TPU:0, one launch (start us, length us, event | category | flops | bytes accessed | tf_op | source)
XLA Modules:
  0.0 151.0 jit_solution(11275907401260138006)
XLA Ops:
  10.7 3.0 %collective-permute-start.1 = (bf16[1,132,1,512]{3,1,2,0:T(8,128)(2,1)S(1)}, bf16[1,132,1,512]{3,1,2,0:T(8,128)(2,1)S(1)}, u32[]{:S(2)}, u32[]{:S(2)}) collective-permute-start(bf16[1,132,1,512]{3,1,2,0:T(8,128)(2,1)S(1)} %bitcast.149), channel_id=1, source_target_pairs={{0,2},{1,3},{2,0},{3,1},{4,6},{5,7},{6,4},{7,5},{8,10},{9,11},{10,... | collective-permute-start | bytes 405512 | tf_op jit(solution)/shard_map/ppermute | solution.py:50
  14.0 1.8 %collective-permute-start.2 = (bf16[1,132,1,512]{3,1,2,0:T(8,128)(2,1)S(1)}, bf16[1,132,1,512]{3,1,2,0:T(8,128)(2,1)S(1)}, u32[]{:S(2)}, u32[]{:S(2)}) collective-permute-start(bf16[1,132,1,512]{3,1,2,0:T(8,128)(2,1)S(1)} %bitcast.153), channel_id=1, source_target_pairs={{0,3},{1,0},{2,1},{3,2},{4,7},{5,4},{6,5},{7,6},{8,11},{9,8},{10,9... | collective-permute-start | bytes 405512 | tf_op jit(solution)/shard_map/ppermute | solution.py:50
  16.0 1.8 %collective-permute-done.1 = bf16[1,132,1,512]{3,1,2,0:T(8,128)(2,1)S(1)} collective-permute-done((bf16[1,132,1,512]{3,1,2,0:T(8,128)(2,1)S(1)}, bf16[1,132,1,512]{3,1,2,0:T(8,128)(2,1)S(1)}, u32[]{:S(2)}, u32[]{:S(2)}) %collective-permute-start.1) | collective-permute-done | bytes 135200 | tf_op jit(solution)/shard_map/ppermute | solution.py:50
  18.0 1.9 %collective-permute-done = bf16[1,132,1,512]{3,1,2,0:T(8,128)(2,1)S(1)} collective-permute-done((bf16[1,132,1,512]{3,1,2,0:T(8,128)(2,1)S(1)}, bf16[1,132,1,512]{3,1,2,0:T(8,128)(2,1)S(1)}, u32[]{:S(2)}, u32[]{:S(2)}) %collective-permute-start) | collective-permute-done | bytes 135200 | tf_op jit(solution)/shard_map/ppermute | solution.py:50
  21.7 2.0 %copy.217 = bf16[8,1,4,36,768]{4,0,3,2,1:T(8,128)(2,1)S(1)} copy(bf16[8,1,4,36,768]{4,2,3,1,0:T(4,128)(2,1)} %param.8) | data formatting | bytes 3538944 | tf_op args[3]
  25.6 38.8 %collective-permute-done.3 = bf16[8,1,4,36,768]{4,0,3,2,1:T(8,128)(2,1)S(1)} collective-permute-done((bf16[8,1,4,36,768]{4,0,3,2,1:T(8,128)(2,1)S(1)}, bf16[8,1,4,36,768]{4,0,3,2,1:T(8,128)(2,1)S(1)}, u32[]{:S(2)}, u32[]{:S(2)}) %collective-permute-start.3) | collective-permute-done | bytes 1769504 | tf_op jit(solution)/shard_map/ppermute | solution.py:32
  64.4 2.3 %pad_maximum_fusion = bf16[8,2,4,36,768]{4,0,3,2,1:T(8,128)(2,1)} fusion(bf16[8,1,4,36,768]{4,0,3,2,1:T(8,128)(2,1)S(1)} %collective-permute-done.3, bf16[8,1,4,36,768]{4,0,3,2,1:T(8,128)(2,1)S(1)} %copy.217), kind=kLoop, calls=%fused_computation.15 | loop fusion | flops 1769472 | bytes 7077888 | tf_op jit(solution)/shard_map/concatenate | solution.py:34
  66.7 3.6 %all-gather.2.cloned.1.call-done = bf16[4,4,132,512]{3,1,2,0:T(4,128)(2,1)} async-done(((bf16[1,4,132,512]{3,1,2,0:T(4,128)(2,1)}), bf16[4,4,132,512]{3,1,2,0:T(4,128)(2,1)}) %all-gather.2.cloned.1.call-update) | async-done | bytes 2162704 | tf_op jit(solution)/shard_map/all_gather | solution.py:54
  70.3 2.0 %copy.211 = bf16[4,4,132,512]{3,2,1,0:T(8,128)(2,1)S(1)} copy(bf16[4,4,132,512]{3,1,2,0:T(4,128)(2,1)} %all-gather.2.cloned.1.call-done) | data formatting | bytes 4325376 | tf_op jit(solution)/shard_map/all_gather | solution.py:54
  75.8 1.5 %convolution_convert_fusion.1 = bf16[16,8,36,512]{3,2,1,0:T(8,128)(2,1)S(1)} fusion(bf16[16,132,512]{2,1,0:T(8,128)(2,1)S(1)} %bitcast.141, s32[16,8,128]{2,1,0:T(8,128)S(1)} %convolution_convert_fusion.2, pred[16,8,128]{2,1,0:T(8,128)(4,1)S(1)} %bitcast.147), kind=kOutput, calls=%fused_computation.17 | convolution fusion | flops 607518720 | bytes 6897664 | tf_op jit(solution)/shard_map/blct,btd->blcd/dot_general | solution.py:75
  77.3 3.1 %convolution_convert_fusion = bf16[16,8,36,512]{3,2,1,0:T(8,128)(2,1)S(1)} fusion(bf16[16,132,512]{2,1,0:T(8,128)(2,1)} %bitcast.142, bf16[16,8,128]{2,1,0:T(8,128)(2,1)S(1)} %bitcast.155, s32[16,8,128]{2,1,0:T(8,128)S(1)} %convolution_convert_fusion.2, pred[16,8,128]{2,1,0:T(8,128)(4,1)S(1)} %bitcast.148), kind=kOutput, calls=%fused_computation.16 | convolution fusion | flops 608108544 | bytes 6930432 | tf_op jit(solution)/shard_map/blct,btd->blcd/dot_general | solution.py:78
  80.4 4.1 %constant_dynamic-slice_fusion = (bf16[4,1,8,36,512]{4,3,2,1,0:T(8,128)(2,1)}, bf16[4,1,8,36,512]{4,3,2,1,0:T(8,128)(2,1)}, bf16[4,1,8,36,512]{4,3,2,1,0:T(8,128...) fusion(bf16[4,4,8,36,512]{4,3,2,1,0:T(8,128)(2,1)S(1)} %bitcast, ...), kind=kLoop, calls=%fused_computation.87 | loop fusion | bytes 18874384 | tf_op jit(solution)/shard_map/jit(dynamic_index_in_dim)/dynamic_slice | solution.py:88
  84.5 5.0 %fusion.12 = f32[4,8,36]{2,0,1:T(4,128)S(1)} fusion(bf16[4,1,8,36,512]{4,3,2,1,0:T(8,128)(2,1)} %get-tuple-element.21, bf16[8,4,36,768]{3,1,2,0:T(4,128)(2,1)} %bitcast.145, bf16[8,768,512]{2,1,0:T(8,128)(2,1)} %param.9), kind=kOutput, calls=%fused_computation.25 | convolution fusion | flops 907737984 | bytes 9245184 | tf_op jit(solution)/shard_map/lscf,lfd->slcd/dot_general | solution.py:95
  90.8 4.3 %fusion.11 = f32[4,8,36]{2,0,1:T(4,128)S(1)} fusion(bf16[4,1,8,36,512]{4,3,2,1,0:T(8,128)(2,1)S(1)} %copy-done.9, bf16[8,1,4,36,768]{4,0,3,2,1:T(8,128)(2,1)S(1)} %copy-done.3, bf16[8,768,512]{2,1,0:T(8,128)(2,1)} %param.9), kind=kOutput, calls=%fused_computation.23 | convolution fusion | flops 907737984 | bytes 9245184 | tf_op jit(solution)/shard_map/lscf,lfd->slcd/dot_general | solution.py:95
  95.8 4.6 %fusion.22 = bf16[8,512,768,1]{2,1,3,0:T(8,128)(2,1)} fusion(bf16[8,4,36,768]{3,1,2,0:T(4,128)(2,1)S(1)} %bitcast.146, bf16[4,1,8,36,512]{4,3,2,1,0:T(8,128)(2,1)S(1)} %copy-done.8), kind=kOutput, calls=%fused_computation.43 | convolution fusion | flops 905969664 | bytes 9240576 | tf_op jit(solution)/shard_map/lscf,slcd->lfd/dot_general | solution.py:90
  100.4 2.3 %fusion.59 = (bf16[8,1,4,36,768]{4,0,3,2,1:T(8,128)(2,1)S(1)}, bf16[8,1,4,36,768]{4,0,3,2,1:T(8,128)(2,1)S(1)}) fusion(bf16[8,2,4,36,768]{4,0,3,2,1:T(8,128)(2,1)} %collective-permute-done.4), kind=kLoop, calls=%fused_computation.101 | loop fusion | bytes 7077888 | tf_op jit(solution)/shard_map/slice | solution.py:36
  102.8 1.7 %fusion.9 = f32[4,8,36]{2,0,1:T(4,128)S(1)} fusion(bf16[4,1,8,36,512]{4,3,2,1,0:T(8,128)(2,1)S(1)} %copy-done.7, bf16[8,768,512]{2,1,0:T(8,128)(2,1)S(1)} %bitcast.162, bf16[8,1,4,36,768]{4,0,3,2,1:T(8,128)(2,1)S(1)} %get-tuple-element.26), kind=kOutput, calls=%fused_computation.19 | convolution fusion | flops 907737984 | bytes 9245184 | tf_op jit(solution)/shard_map/lscf,lfd->slcd/dot_general | solution.py:95
  104.6 1.6 %fusion.10 = f32[4,8,36]{2,0,1:T(4,128)S(1)} fusion(bf16[4,1,8,36,512]{4,3,2,1,0:T(8,128)(2,1)S(1)} %copy-done.6, bf16[8,768,512]{2,1,0:T(8,128)(2,1)S(1)} %bitcast.162, bf16[8,1,4,36,768]{4,0,3,2,1:T(8,128)(2,1)S(1)} %get-tuple-element.27), kind=kOutput, calls=%fused_computation.21 | convolution fusion | flops 907737984 | bytes 9245184 | tf_op jit(solution)/shard_map/lscf,lfd->slcd/dot_general | solution.py:95
  107.4 1.6 %reshape.86 = f32[16,1,288]{2,1,0:T(1,128)} reshape(f32[16,8,36]{2,1,0:T(8,128)} %bitcast.49) | data formatting | bytes 36864
  109.0 4.1 %all-to-all-start = ((f32[16,1,288]{2,1,0:T(1,128)}), f32[16,1,288]{2,1,0:T(1,128)}, u32[]{:S(2)}, u32[]{:S(2)}) async-start(f32[16,1,288]{2,1,0:T(1,128)} %reshape.86), calls=%async_computation | async-start | bytes 49152 | tf_op jit(solution)/shard_map/all_to_all | solution.py:99
  113.1 3.4 %fusion.17 = bf16[8,768,512,1]{1,2,3,0:T(8,128)(2,1)S(1)} fusion(bf16[8,1,4,36,768]{4,0,3,2,1:T(8,128)(2,1)S(1)} %get-tuple-element.27, bf16[4,1,8,36,512]{4,3,2,1,0:T(8,128)(2,1)} %get-tuple-element.36), kind=kOutput, calls=%fused_computation.38 | convolution fusion | flops 905969664 | bytes 9240576 | tf_op jit(solution)/shard_map/lscf,slcd->lfd/dot_general | solution.py:90
  116.5 1.9 %fusion.18 = bf16[8,768,512,1]{1,2,3,0:T(8,128)(2,1)S(1)} fusion(bf16[8,1,4,36,768]{4,0,3,2,1:T(8,128)(2,1)S(1)} %get-tuple-element.26, bf16[4,1,8,36,512]{4,3,2,1,0:T(8,128)(2,1)S(1)} %copy-done.1), kind=kOutput, calls=%fused_computation.39 | convolution fusion | flops 905969664 | bytes 9240576 | tf_op jit(solution)/shard_map/lscf,slcd->lfd/dot_general | solution.py:90
  118.4 9.5 %fusion = f32[8,768,512]{1,2,0:T(8,128)} fusion(bf16[8,512,768,1]{2,1,3,0:T(8,128)(2,1)} %fusion.22, bf16[8,768,512,1]{1,2,3,0:T(8,128)(2,1)S(1)} %fusion.17, bf16[8,768,512,1]{1,2,3,0:T(8,128)(2,1)S(1)} %fusion.18, bf16[8,1,4,36,768]{4,0,3,2,1:T(8,128)(2,1)S(1)} %copy-done.4, bf16[4,1,8,36,512]{4,3,2,1,0:T(8,128)(2,1)} %get-tuple-element.38), kind=kOutput, calls=%fused_computation.3 | convolution fusion | flops 931135488 | bytes 34406400 | tf_op jit(solution)/shard_map/lscf,slcd->lfd/dot_general | solution.py:90
  127.9 12.6 %copy.237 = f32[8,768,512]{2,1,0:T(8,128)} copy(f32[8,768,512]{1,2,0:T(8,128)} %fusion) | data formatting | bytes 25165824
  (82 shorter events, 17.8 us)
Async XLA Ops:
  7.2 63.2 %all-gather.2.cloned.1.call-start = ((), (), s32[]{:S(2)}) async-start(), calls=%async_computation.1 | async-start | bytes 2703360 | tf_op jit(solution)/shard_map/all_gather | solution.py:54
  10.7 7.1 %collective-permute-start.1 = (bf16[1,132,1,512]{3,1,2,0:T(8,128)(2,1)S(1)}, bf16[1,132,1,512]{3,1,2,0:T(8,128)(2,1)S(1)}, u32[]{:S(2)}, u32[]{:S(2)}) collective-permute-start(bf16[1,132,1,512]{3,1,2,0:T(8,128)(2,1)S(1)} %bitcast.149), channel_id=1, source_target_pairs={{0,2},{1,3},{2,0},{3,1},{4,6},{5,7},{6,4},{7,5},{8,10},{9,11},{10,... | collective-permute-start | bytes 405512 | tf_op jit(solution)/shard_map/ppermute | solution.py:50
  13.9 6.1 %collective-permute-start = (bf16[1,132,1,512]{3,1,2,0:T(8,128)(2,1)S(1)}, bf16[1,132,1,512]{3,1,2,0:T(8,128)(2,1)S(1)}, u32[]{:S(2)}, u32[]{:S(2)}) collective-permute-start(bf16[1,132,1,512]{3,1,2,0:T(8,128)(2,1)S(1)} %bitcast.151), channel_id=1, source_target_pairs={{0,1},{1,2},{2,3},{3,0},{4,5},{5,6},{6,7},{7,4},{8,9},{9,10},{10,1... | collective-permute-start | bytes 405512 | tf_op jit(solution)/shard_map/ppermute | solution.py:50
  14.0 6.0 %collective-permute-start.2 = (bf16[1,132,1,512]{3,1,2,0:T(8,128)(2,1)S(1)}, bf16[1,132,1,512]{3,1,2,0:T(8,128)(2,1)S(1)}, u32[]{:S(2)}, u32[]{:S(2)}) collective-permute-start(bf16[1,132,1,512]{3,1,2,0:T(8,128)(2,1)S(1)} %bitcast.153), channel_id=1, source_target_pairs={{0,3},{1,0},{2,1},{3,2},{4,7},{5,4},{6,5},{7,6},{8,11},{9,8},{10,9... | collective-permute-start | bytes 405512 | tf_op jit(solution)/shard_map/ppermute | solution.py:50
  21.6 3.1 %copy-start.11 = (s32[128,8]{0,1:T(8,128)S(1)}, s32[128,8]{0,1:T(8,128)}, u32[]{:S(2)}) copy-start(s32[128,8]{0,1:T(8,128)} %param.7) | copy-start | bytes 12292
  23.7 40.7 %collective-permute-start.3 = (bf16[8,1,4,36,768]{4,0,3,2,1:T(8,128)(2,1)S(1)}, bf16[8,1,4,36,768]{4,0,3,2,1:T(8,128)(2,1)S(1)}, u32[]{:S(2)}, u32[]{:S(2)}) collective-permute-start(bf16[8,1,4,36,768]{4,0,3,2,1:T(8,128)(2,1)S(1)} %copy.217), channel_id=1, source_target_pairs={{0,2},{1,3},{2,0},{3,1},{4,6},{5,7},{6,4},{7,5},{8,10},{9,11},{10,... | collective-permute-start | bytes 5308424 | tf_op jit(solution)/shard_map/ppermute | solution.py:32
  64.4 2.4 %copy-start.2 = (bf16[8,1,4,36,768]{4,0,3,2,1:T(8,128)(2,1)}, bf16[8,1,4,36,768]{4,0,3,2,1:T(8,128)(2,1)S(1)}, u32[]{:S(2)}) copy-start(bf16[8,1,4,36,768]{4,0,3,2,1:T(8,128)(2,1)S(1)} %collective-permute-done.3) | copy-start | bytes 5308420
  66.7 33.7 %collective-permute-start.4 = (bf16[8,2,4,36,768]{4,0,3,2,1:T(8,128)(2,1)}, bf16[8,2,4,36,768]{4,0,3,2,1:T(8,128)(2,1)}, u32[]{:S(2)}, u32[]{:S(2)}) collective-permute-start(bf16[8,2,4,36,768]{4,0,3,2,1:T(8,128)(2,1)} %pad_maximum_fusion), channel_id=1, source_target_pairs={{0,1},{1,0},{2,3},{3,2},{4,5},{5,4},{6,7},{7,6},{8,9},{9,8},{10,11... | collective-permute-start | bytes 10616840 | tf_op jit(solution)/shard_map/ppermute | solution.py:33
  72.4 3.4 %copy-start = (bf16[4,4,132,512]{3,2,1,0:T(8,128)(2,1)}, bf16[4,4,132,512]{3,2,1,0:T(8,128)(2,1)S(1)}, u32[]{:S(2)}) copy-start(bf16[4,4,132,512]{3,2,1,0:T(8,128)(2,1)S(1)} %copy.211) | copy-start | bytes 6488068
  84.5 6.3 %copy-start.3 = (bf16[8,1,4,36,768]{4,0,3,2,1:T(8,128)(2,1)S(1)}, bf16[8,1,4,36,768]{4,0,3,2,1:T(8,128)(2,1)}, u32[]{:S(2)}) copy-start(bf16[8,1,4,36,768]{4,0,3,2,1:T(8,128)(2,1)} %copy-done.2) | copy-start | bytes 5308420
  84.5 6.3 %copy-start.9 = (bf16[4,1,8,36,512]{4,3,2,1,0:T(8,128)(2,1)S(1)}, bf16[4,1,8,36,512]{4,3,2,1,0:T(8,128)(2,1)}, u32[]{:S(2)}) copy-start(bf16[4,1,8,36,512]{4,3,2,1,0:T(8,128)(2,1)} %get-tuple-element.20) | copy-start | bytes 3538948
  90.8 5.0 %copy-start.5 = (bf16[8,1,4,36,768]{4,2,3,1,0:T(4,128)(2,1)S(1)}, bf16[8,1,4,36,768]{4,2,3,1,0:T(4,128)(2,1)}, u32[]{:S(2)}) copy-start(bf16[8,1,4,36,768]{4,2,3,1,0:T(4,128)(2,1)} %param.8) | copy-start | bytes 5308420
  90.8 5.0 %copy-start.8 = (bf16[4,1,8,36,512]{4,3,2,1,0:T(8,128)(2,1)S(1)}, bf16[4,1,8,36,512]{4,3,2,1,0:T(8,128)(2,1)}, u32[]{:S(2)}) copy-start(bf16[4,1,8,36,512]{4,3,2,1,0:T(8,128)(2,1)} %get-tuple-element.35) | copy-start | bytes 3538948
  90.8 12.0 %slice-start = ((s8[6291456]{0:T(1024)(128)(4,1)}), s8[2097152]{0:T(1024)(128)(4,1)S(1)}, s32[]{:S(2)}) async-start(s8[6291456]{0:T(1024)(128)(4,1)} %bitcast.161), calls=%async_computation.2 | async-start | bytes 4194304
  95.8 7.0 %slice-start.1 = ((s8[6291456]{0:T(1024)(128)(4,1)}), s8[4194304]{0:T(1024)(128)(4,1)S(1)}, s32[]{:S(2)}) async-start(s8[6291456]{0:T(1024)(128)(4,1)} %bitcast.161), calls=%async_computation.3 | async-start | bytes 8388608
  100.4 2.4 %copy-start.7 = (bf16[4,1,8,36,512]{4,3,2,1,0:T(8,128)(2,1)S(1)}, bf16[4,1,8,36,512]{4,3,2,1,0:T(8,128)(2,1)}, u32[]{:S(2)}) copy-start(bf16[4,1,8,36,512]{4,3,2,1,0:T(8,128)(2,1)} %get-tuple-element.18) | copy-start | bytes 3538948
  102.8 1.8 %copy-start.6 = (bf16[4,1,8,36,512]{4,3,2,1,0:T(8,128)(2,1)S(1)}, bf16[4,1,8,36,512]{4,3,2,1,0:T(8,128)(2,1)}, u32[]{:S(2)}) copy-start(bf16[4,1,8,36,512]{4,3,2,1,0:T(8,128)(2,1)} %get-tuple-element.19) | copy-start | bytes 3538948
  109.0 31.6 %all-to-all-start = ((f32[16,1,288]{2,1,0:T(1,128)}), f32[16,1,288]{2,1,0:T(1,128)}, u32[]{:S(2)}, u32[]{:S(2)}) async-start(f32[16,1,288]{2,1,0:T(1,128)} %reshape.86), calls=%async_computation | async-start | bytes 49152 | tf_op jit(solution)/shard_map/all_to_all | solution.py:99
  113.1 3.4 %copy-start.1 = (bf16[4,1,8,36,512]{4,3,2,1,0:T(8,128)(2,1)S(1)}, bf16[4,1,8,36,512]{4,3,2,1,0:T(8,128)(2,1)}, u32[]{:S(2)}) copy-start(bf16[4,1,8,36,512]{4,3,2,1,0:T(8,128)(2,1)} %get-tuple-element.37) | copy-start | bytes 3538948
  116.5 2.0 %copy-start.4 = (bf16[8,1,4,36,768]{4,0,3,2,1:T(8,128)(2,1)S(1)}, bf16[8,1,4,36,768]{4,0,3,2,1:T(8,128)(2,1)}, u32[]{:S(2)}) copy-start(bf16[8,1,4,36,768]{4,0,3,2,1:T(8,128)(2,1)} %copy-done.2) | copy-start | bytes 5308420
  127.9 14.8 %copy-start.10 = (pred[128,8,32]{0,2,1:T(8,128)(4,1)S(1)}, pred[128,8,32]{0,2,1:T(8,128)(4,1)}, u32[]{:S(2)}) copy-start(pred[128,8,32]{0,2,1:T(8,128)(4,1)} %get-tuple-element.34) | copy-start | bytes 98308
Sparse Core Ops, SparseCore 0:
  21.8 48.5 all-gather.1
